TPU v7x, 32 devices: a whole 2x2x4 slice. The times are simulated.
32 devices in a mesh: gx: 8 (over z, x), gy: 4 (over y, core).
Axes of the slice: x: 2, y: 2, z: 4, core: 2. Of those that a mesh axis runs over, the one named last changes fastest.
Arguments:
- prior_basis: float32 [128, 128, 128], P('gx', 'gy'), may hold values from -6 to 6
- cond_x: float32 [128, 128], P('gx', 'gy'), may hold values from 0.5 to 5
- cond_y: float32 [128, 128], P('gx', 'gy'), may hold values from 0.5 to 5
- capacitance: float32 [128, 128], P('gx', 'gy'), may hold values from 0.05 to 1
- pad_mask: int32 [128, 128], P('gx', 'gy'), may hold values 0 or 1
- port_nodes: int32 [128], replicated, may hold values from 0 to 16383
Outputs:
- new_basis: float32 [128, 128, 128], P('gx', 'gy')
- reduced_g: float32 [128, 128], replicated
- reduced_c: float32 [128, 128], replicated
Inputs may be any that keep to these rules, and one draw needn't show every extreme that they name: `port_nodes`: a row-major node index into the grid of 128 x 128 nodes.
All inputs are finite; a program needn't handle non-finite values. No bound on the sum of `pad_mask` on one device may be relied on, other than what follows from the above.
Results may differ from a plain program's by a relative error of at most 0.0003.
Values sent between devices are 32-bit elements; how exact they have to be, the bound alone decides.
No kernel may reach another device: no remote copies, remote signals or barrier semaphores. Data moves between devices by JAX's collectives and lax.ppermute only.
A program may use at most 64 MiB of HBM per device.

v0:
```python
import jax
import jax.numpy as jnp
from jax import lax
from jax.sharding import PartitionSpec as P

SWEEPS = 4
shift_point = 0.5
supply_conductance = 4.0
port_current = 8.0
highest = lax.Precision.HIGHEST


def shifted(shard, axis, by):
    devices = lax.axis_size(axis)
    pairs = [(i, i + by) for i in range(devices) if 0 <= i + by < devices]
    return lax.ppermute(shard, axis, pairs)


def padded(cells, sides, width):
    for axis, dim in sides:
        count = lax.axis_size(axis)
        ends = count - 1
        head = lax.slice_in_dim(cells, 0, width, axis=dim)
        tail = lax.slice_in_dim(cells, cells.shape[dim] - width, cells.shape[dim], axis=dim)
        cells = jnp.concatenate(
            [
                lax.ppermute(tail, axis, [(i, (i + 1) % count) for i in range(ends)]),
                cells,
                lax.ppermute(head, axis, [((i + 1) % count, i) for i in range(ends)]),
            ],
            axis=dim,
        )
    return cells


def neighbors(ext, links):
    cx, cy, cx_up, cy_left = links
    total = cx[:, :, None] * ext[2:, 1:-1] + cx_up[:, :, None] * ext[:-2, 1:-1]
    return total + cy[:, :, None] * ext[1:-1, 2:] + cy_left[:, :, None] * ext[1:-1, :-2]


def local_inner(left, right):
    a = left.reshape(-1, left.shape[-1])
    b = right.reshape(-1, right.shape[-1])
    return jnp.einsum("cp,cq->pq", a, b, precision=highest, preferred_element_type=jnp.float32)


def per_device(prior_basis, cond_x, cond_y, capacitance, pad_mask, port_nodes):
    rows_dev, cols_dev = cond_x.shape
    width = port_nodes.shape[0]
    count_x = lax.axis_size("gx")
    count_y = lax.axis_size("gy")
    total_rows = rows_dev * count_x
    total_cols = cols_dev * count_y
    nodes = total_rows * total_cols
    row_start = lax.axis_index("gx") * rows_dev
    col_start = lax.axis_index("gy") * cols_dev
    global_rows = row_start + jnp.arange(rows_dev, dtype=jnp.int32)[:, None]
    global_cols = col_start + jnp.arange(cols_dev, dtype=jnp.int32)[None, :]
    cx = jnp.where(global_rows < total_rows - 1, cond_x, jnp.float32(0.0))
    cy = jnp.where(global_cols < total_cols - 1, cond_y, jnp.float32(0.0))
    above = shifted(cx[-1:, :], "gx", 1)
    beside = shifted(cy[:, -1:], "gy", 1)
    cx_up = jnp.concatenate([above, cx[:-1]], axis=0)
    cy_left = jnp.concatenate([beside, cy[:, :-1]], axis=1)
    links = (cx, cy, cx_up, cy_left)
    diag_g = cx + cx_up + cy + cy_left + supply_conductance * pad_mask.astype(jnp.float32)
    diag = (diag_g + shift_point * capacitance)[:, :, None]
    node_ids = global_rows * total_cols + global_cols
    onehot = (node_ids[:, :, None] == port_nodes[None, None, :]).astype(jnp.float32)
    rhs = capacitance[:, :, None] * prior_basis + port_current * onehot

    def sweep(step, current):
        ext = padded(current, (("gx", 0), ("gy", 1)), 1)
        return (rhs + neighbors(ext, links)) / diag

    field = lax.fori_loop(0, SWEEPS, sweep, rhs / diag)
    proj = lax.psum(local_inner(prior_basis, field), ("gx", "gy")) / nodes
    cand = field - jnp.einsum("xyk,kp->xyp", prior_basis, proj, precision=highest)
    gram = lax.psum(local_inner(cand, cand), ("gx", "gy")) / nodes
    lower = jnp.linalg.cholesky(gram)
    flat = cand.reshape(-1, width)
    basis_flat = lax.linalg.triangular_solve(
        lower, flat, left_side=False, lower=True, transpose_a=True
    )
    new_basis = basis_flat.reshape(rows_dev, cols_dev, width)
    ext = padded(new_basis, (("gx", 0), ("gy", 1)), 1)
    g_image = diag_g[:, :, None] * new_basis - neighbors(ext, links)
    g_raw, c_raw = lax.psum(
        (
            local_inner(new_basis, g_image),
            local_inner(new_basis, capacitance[:, :, None] * new_basis),
        ),
        ("gx", "gy"),
    )
    reduced_g = g_raw / nodes
    reduced_c = c_raw / nodes
    return (new_basis, reduced_g, reduced_c)


def solution(mesh):
    placed = (P("gx", "gy", None), P("gx", "gy"), P("gx", "gy"), P("gx", "gy"), P("gx", "gy"), P())
    return jax.shard_map(
        per_device,
        mesh=mesh,
        in_specs=placed,
        out_specs=(P("gx", "gy", None), P(), P()),
        check_vma=False,
    )
```

profile of v0, /device:TPU:0, one launch (start us, length us, event | category | flops | bytes accessed | tf_op | source)
XLA Modules:
  0.0 506.1 jit_solution(9967310550308028480)
XLA Ops:
  7.9 2.5 collective-permute-start.5
  10.5 4.2 collective-permute-start.4
  18.0 68.9 %while.10 = (s32[]{:T(128)}, f32[16,32,128]{2,1,0:T(8,128)S(1)}, f32[16,32]{1,0:T(8,128)S(1)}, f32[16,32]{1,0:T(8,128)S(1)}, f32[16,32]{1,0:T(8,128)S(1)}, /*ind...) while((s32[]{:T(128)}, f32[16,32,128]{2,1,0:T(8,128)S(1)}, ...), condition=%wide.region_1.2_spmd, body=%wide.region_0.1_spmd.sunk | while | flops 851970 | bytes 2564349 | solution.py:77
  18.1 4.3 collective-permute-start
  23.8 4.6 collective-permute-done.1
  31.2 3.6 collective-permute-done.3
  35.2 4.8 collective-permute-start
  41.5 4.2 collective-permute-done.1
  45.7 2.9 collective-permute-start.2
  49.9 2.7 collective-permute-done.3
  53.1 2.9 collective-permute-start
  57.5 4.2 collective-permute-done.1
  61.7 3.2 collective-permute-start.2
  69.1 4.8 collective-permute-start
  75.4 4.2 collective-permute-done.1
  79.6 2.9 collective-permute-start.2
  83.8 2.7 collective-permute-done.3
  88.3 117.4 %all-reduce.5.cloned.1.call-done = f32[128,128]{0,1:T(8,128)} async-done(((f32[128,128]{0,1:T(8,128)}), f32[128,128]{0,1:T(8,128)}) %all-reduce.5.cloned.1.call-update) | async-done | bytes 65552 | tf_op jit(solution)/shard_map/psum | solution.py:78
  208.2 122.0 %all-reduce.7.cloned.1.call-done = f32[128,128]{0,1:T(8,128)} async-done(((f32[128,128]{0,1:T(8,128)}), f32[128,128]{0,1:T(8,128)}) %all-reduce.7.cloned.1.call-update) | async-done | bytes 65552 | tf_op jit(solution)/shard_map/psum | solution.py:80
  331.9 11.7 %cholesky.16 = f32[128,128]{1,0:T(8,128)S(1)} custom-call(f32[128,128]{1,0:T(8,128)S(1)} %fusion.24), custom_call_target="Cholesky" | custom-call | tf_op jit(solution)/shard_map/jit(cholesky)/cholesky | solution.py:81
  345.0 9.8 %custom-call.6 = f32[1,128,128]{1,2,0:T(8,128)S(1)} custom-call(f32[1,128,128]{2,1,0:T(8,128)S(1)} %fusion.21), custom_call_target="InvertDiagBlocksLowerTriangular" | custom-call | tf_op jit(solution)/shard_map/triangular_solve | solution.py:83
  356.5 4.5 collective-permute-start.7
  363.8 3.0 collective-permute-start.9
  369.8 127.4 %all-reduce.9.cloned.1.call-done = (f32[128,128]{0,1:T(8,128)}, f32[128,128]{0,1:T(8,128)}) async-done(((f32[128,128]{0,1:T(8,128)}, f32[128,128]{0,1:T(8,128)}), (f32[128,128]{0,1:T(8,128)}, f32[128,128]{0,1:T(8,128)})) %all-reduce.9.cloned.1.call-update) | async-done | bytes 131088 | tf_op jit(solution)/shard_map/psum | solution.py:89
  (106 shorter events, 37.2 us)
Async XLA Ops:
  7.2 198.5 %all-reduce.5.cloned.1.call-start = ((), (), s32[]{:S(2)}) async-start(), calls=%async_computation | async-start | bytes 131072 | tf_op jit(solution)/shard_map/psum | solution.py:78
  7.9 6.9 %collective-permute-start.5 = (f32[16,1]{1,0:T(8,128)S(1)}, f32[16,1]{1,0:T(8,128)S(1)}, u32[]{:S(2)}, u32[]{:S(2)}) collective-permute-start(f32[16,1]{1,0:T(8,128)S(1)} %slice.102), channel_id=1, source_target_pairs={{0,1},{1,2},{2,3},{4,5},{5,6},{6,7},{8,9},{9,10},{10,11},{12,13},{... | collective-permute-start | bytes 200 | tf_op jit(solution)/shard_map/ppermute | solution.py:16
  10.5 5.5 %collective-permute-start.4 = (f32[1,32]{1,0:T(1,128)S(1)}, f32[1,32]{1,0:T(1,128)S(1)}, u32[]{:S(2)}, u32[]{:S(2)}) collective-permute-start(f32[1,32]{1,0:T(1,128)S(1)} %slice.100), channel_id=1, source_target_pairs={{0,4},{4,8},{8,12},{12,16},{16,20},{20,24},{24,28},{1,5},{5,9},{9,... | collective-permute-start | bytes 392 | tf_op jit(solution)/shard_map/ppermute | solution.py:16
  18.1 5.7 %collective-permute-start = (f32[1,32,128]{2,1,0:T(8,128)S(1)}, f32[1,32,128]{2,1,0:T(8,128)S(1)}, u32[]{:S(2)}, u32[]{:S(2)}) collective-permute-start(f32[1,32,128]{2,1,0:T(8,128)S(1)} %get-tuple-element.136), channel_id=1, source_target_pairs={{0,4},{4,8},{8,12},{12,16},{16,20},{20,24},{24,28},{1,5},{5,9},{9,... | collective-permute-start | bytes 49160 | tf_op jit(solution)/shard_map/while/body/eval_jaxpr/ppermute | solution.py:27
  22.4 6.1 %collective-permute-start.1 = (f32[1,32,128]{2,1,0:T(8,128)S(1)}, f32[1,32,128]{2,1,0:T(8,128)S(1)}, u32[]{:S(2)}, u32[]{:S(2)}) collective-permute-start(f32[1,32,128]{2,1,0:T(8,128)S(1)} %get-tuple-element.137), channel_id=1, source_target_pairs={{4,0},{8,4},{12,8},{16,12},{20,16},{24,20},{28,24},{5,1},{9,5},{13... | collective-permute-start | bytes 49160 | tf_op jit(solution)/shard_map/while/body/eval_jaxpr/ppermute | solution.py:29
  29.9 4.9 collective-permute-start.3
  35.2 6.3 %collective-permute-start = (f32[1,32,128]{2,1,0:T(8,128)S(1)}, f32[1,32,128]{2,1,0:T(8,128)S(1)}, u32[]{:S(2)}, u32[]{:S(2)}) collective-permute-start(f32[1,32,128]{2,1,0:T(8,128)S(1)} %get-tuple-element.136), channel_id=1, source_target_pairs={{0,4},{4,8},{8,12},{12,16},{16,20},{20,24},{24,28},{1,5},{5,9},{9,... | collective-permute-start | bytes 49160 | tf_op jit(solution)/shard_map/while/body/eval_jaxpr/ppermute | solution.py:27
  40.1 5.6 %collective-permute-start.1 = (f32[1,32,128]{2,1,0:T(8,128)S(1)}, f32[1,32,128]{2,1,0:T(8,128)S(1)}, u32[]{:S(2)}, u32[]{:S(2)}) collective-permute-start(f32[1,32,128]{2,1,0:T(8,128)S(1)} %get-tuple-element.137), channel_id=1, source_target_pairs={{4,0},{8,4},{12,8},{16,12},{20,16},{24,20},{28,24},{5,1},{9,5},{13... | collective-permute-start | bytes 49160 | tf_op jit(solution)/shard_map/while/body/eval_jaxpr/ppermute | solution.py:29
  45.7 4.2 collective-permute-start.2
  48.6 4.0 collective-permute-start.3
  53.1 4.4 collective-permute-start
  56.1 5.6 %collective-permute-start.1 = (f32[1,32,128]{2,1,0:T(8,128)S(1)}, f32[1,32,128]{2,1,0:T(8,128)S(1)}, u32[]{:S(2)}, u32[]{:S(2)}) collective-permute-start(f32[1,32,128]{2,1,0:T(8,128)S(1)} %get-tuple-element.137), channel_id=1, source_target_pairs={{4,0},{8,4},{12,8},{16,12},{20,16},{24,20},{28,24},{5,1},{9,5},{13... | collective-permute-start | bytes 49160 | tf_op jit(solution)/shard_map/while/body/eval_jaxpr/ppermute | solution.py:29
  61.7 4.5 collective-permute-start.2
  64.9 3.8 collective-permute-start.3
  69.1 6.3 %collective-permute-start = (f32[1,32,128]{2,1,0:T(8,128)S(1)}, f32[1,32,128]{2,1,0:T(8,128)S(1)}, u32[]{:S(2)}, u32[]{:S(2)}) collective-permute-start(f32[1,32,128]{2,1,0:T(8,128)S(1)} %get-tuple-element.136), channel_id=1, source_target_pairs={{0,4},{4,8},{8,12},{12,16},{16,20},{20,24},{24,28},{1,5},{5,9},{9,... | collective-permute-start | bytes 49160 | tf_op jit(solution)/shard_map/while/body/eval_jaxpr/ppermute | solution.py:27
  73.9 5.6 %collective-permute-start.1 = (f32[1,32,128]{2,1,0:T(8,128)S(1)}, f32[1,32,128]{2,1,0:T(8,128)S(1)}, u32[]{:S(2)}, u32[]{:S(2)}) collective-permute-start(f32[1,32,128]{2,1,0:T(8,128)S(1)} %get-tuple-element.137), channel_id=1, source_target_pairs={{4,0},{8,4},{12,8},{16,12},{20,16},{24,20},{28,24},{5,1},{9,5},{13... | collective-permute-start | bytes 49160 | tf_op jit(solution)/shard_map/while/body/eval_jaxpr/ppermute | solution.py:29
  79.6 4.2 collective-permute-start.2
  82.5 4.0 collective-permute-start.3
  88.2 242.0 %all-reduce.7.cloned.1.call-start = ((), (), s32[]{:S(2)}) async-start(), calls=%async_computation.1 | async-start | bytes 131072 | tf_op jit(solution)/shard_map/psum | solution.py:80
  208.2 289.1 %all-reduce.9.cloned.1.call-start = ((), (), s32[]{:S(2)}) async-start(), calls=%async_computation.2 | async-start | bytes 262144 | tf_op jit(solution)/shard_map/psum | solution.py:89
  355.2 5.9 %collective-permute-start.6 = (f32[1,32,128]{2,1,0:T(8,128)S(1)}, f32[1,32,128]{2,1,0:T(8,128)S(1)}, u32[]{:S(2)}, u32[]{:S(2)}) collective-permute-start(f32[1,32,128]{2,1,0:T(8,128)S(1)} %get-tuple-element.80), channel_id=1, source_target_pairs={{4,0},{8,4},{12,8},{16,12},{20,16},{24,20},{28,24},{5,1},{9,5},{13... | collective-permute-start | bytes 49160 | tf_op jit(solution)/shard_map/ppermute | solution.py:29
  356.5 6.0 %collective-permute-start.7 = (f32[1,32,128]{2,1,0:T(8,128)S(1)}, f32[1,32,128]{2,1,0:T(8,128)S(1)}, u32[]{:S(2)}, u32[]{:S(2)}) collective-permute-start(f32[1,32,128]{2,1,0:T(8,128)S(1)} %get-tuple-element.79), channel_id=1, source_target_pairs={{0,4},{4,8},{8,12},{12,16},{16,20},{20,24},{24,28},{1,5},{5,9},{9,... | collective-permute-start | bytes 49160 | tf_op jit(solution)/shard_map/ppermute | solution.py:27
  362.5 5.7 %collective-permute-start.8 = (f32[18,1,128]{2,1,0:T(1,128)S(1)}, f32[18,1,128]{2,1,0:T(1,128)S(1)}, u32[]{:S(2)}, u32[]{:S(2)}) collective-permute-start(f32[18,1,128]{2,1,0:T(1,128)S(1)} %get-tuple-element.77), channel_id=1, source_target_pairs={{1,0},{2,1},{3,2},{5,4},{6,5},{7,6},{9,8},{10,9},{11,10},{13,12},{... | collective-permute-start | bytes 27656 | tf_op jit(solution)/shard_map/ppermute | solution.py:29
  363.8 4.4 collective-permute-start.9
  (9 other events, 92.3 us)
Sparse Core Ops, SparseCore 0:
  88.3 117.3 all-reduce.4
  211.8 118.3 all-reduce.6
  369.9 127.2 all-reduce.8
where the time goes:
time: 507 us; the launch traced here: 506 us
  waiting for transfers between devices  399 us (79%)
  starting transfers between devices  54.5 us (11%)
  other arithmetic  28.1 us (6%)
  between operations  14 us (3%)
  matrix products  6.58 us (1%)
    psum x1, waiting for transfers between devices, per_device(): lax.psum((local_inner(new_basis, g_image), local_inner(new_basis, capacit...  127 us
    psum x1, waiting for transfers between devices, per_device(): gram = lax.psum(local_inner(cand, cand), ('gx', 'gy')) / nodes  122 us
    psum x1, waiting for transfers between devices, per_device(): proj = lax.psum(local_inner(prior_basis, field), ('gx', 'gy')) / nodes  117 us
    ppermute x10, starting transfers between devices, padded(): lax.ppermute(tail, axis, [(i, (i + 1) % count) for i in range(ends)])  34.8 us
    ppermute x10, waiting for transfers between devices, padded(): lax.ppermute(head, axis, [((i + 1) % count, i) for i in range(ends)])  28.7 us
    ppermute x10, starting transfers between devices, padded(): lax.ppermute(head, axis, [((i + 1) % count, i) for i in range(ends)])  12.9 us
    another operation x3, other arithmetic, per_device(): lower = jnp.linalg.cholesky(gram)  12.4 us
    another operation x2, other arithmetic, per_device(): lax.linalg.triangular_solve(lower, flat, left_side=False, lower=True, tra...  10.5 us
  transfers between devices with their start and end apart: 25, of which 17 were waited for; matrix products, arithmetic and copies ran while one was open for 0% of the time, Pallas kernels for 0%

commit v1 on v0

--- a/solution.py
+++ b/solution.py
@@ -86,12 +86,19 @@
     new_basis = basis_flat.reshape(rows_dev, cols_dev, width)
     ext = padded(new_basis, (("gx", 0), ("gy", 1)), 1)
     g_image = diag_g[:, :, None] * new_basis - neighbors(ext, links)
-    g_raw, c_raw = lax.psum(
+
+    def connect_tracks(arr_in):
+        axis_key = "gx"
+        which_axis = "gy"
+        for j in (which_axis, axis_key):
+            arr_in = lax.psum(arr_in, j)
+        return arr_in
+
+    g_raw, c_raw = connect_tracks(
         (
             local_inner(new_basis, g_image),
             local_inner(new_basis, capacitance[:, :, None] * new_basis),
-        ),
-        ("gx", "gy"),
+        )
     )
     reduced_g = g_raw / nodes
     reduced_c = c_raw / nodes

time: 507 us -> 489 us (0.964)
  waiting for transfers between devices: 399 us -> 381 us
    psum x1 -> x2, waiting for transfers between devices: 127 us -> 110 us  [connect_tracks(): arr_in = lax.psum(arr_in, j)]
  transfers between devices with their start and end apart: 25 -> 26, of which waited for: 17 -> 18; matrix products, arithmetic and copies ran while one was open for 0% -> 0% of each run, Pallas kernels for 0% -> 0%
where the time goes in v1:
time: 489 us; the launch traced here: 488 us
  waiting for transfers between devices  381 us (78%)
  starting transfers between devices  54.6 us (11%)
  other arithmetic  28.1 us (6%)
  between operations  14 us (3%)
  matrix products  6.59 us (1%)
    psum x1, waiting for transfers between devices, per_device(): gram = lax.psum(local_inner(cand, cand), ('gx', 'gy')) / nodes  122 us
    psum x1, waiting for transfers between devices, per_device(): proj = lax.psum(local_inner(prior_basis, field), ('gx', 'gy')) / nodes  117 us
    psum x2, waiting for transfers between devices, connect_tracks(): arr_in = lax.psum(arr_in, j)  110 us
    ppermute x10, starting transfers between devices, padded(): lax.ppermute(tail, axis, [(i, (i + 1) % count) for i in range(ends)])  34.8 us
    ppermute x10, waiting for transfers between devices, padded(): lax.ppermute(head, axis, [((i + 1) % count, i) for i in range(ends)])  28.7 us
    ppermute x10, starting transfers between devices, padded(): lax.ppermute(head, axis, [((i + 1) % count, i) for i in range(ends)])  12.9 us
    another operation x3, other arithmetic, per_device(): lower = jnp.linalg.cholesky(gram)  12.4 us
    another operation x2, other arithmetic, per_device(): lax.linalg.triangular_solve(lower, flat, left_side=False, lower=True, tra...  10.5 us
  transfers between devices with their start and end apart: 26, of which 18 were waited for; matrix products, arithmetic and copies ran while one was open for 0% of the time, Pallas kernels for 0%

profile of v1, /device:TPU:0, one launch (start us, length us, event | category | flops | bytes accessed | tf_op | source)
XLA Modules:
  0.0 488.4 jit_solution(14497406423800087461)
XLA Ops:
  10.5 4.2 collective-permute-start.4
  18.0 68.9 %while.10 = (s32[]{:T(128)}, f32[16,32,128]{2,1,0:T(8,128)S(1)}, f32[16,32]{1,0:T(8,128)S(1)}, f32[16,32]{1,0:T(8,128)S(1)}, f32[16,32]{1,0:T(8,128)S(1)}, /*ind...) while((s32[]{:T(128)}, f32[16,32,128]{2,1,0:T(8,128)S(1)}, ...), condition=%wide.region_1.2_spmd, body=%wide.region_0.1_spmd.sunk | while | flops 851970 | bytes 2564349 | solution.py:77
  18.1 4.3 collective-permute-start
  23.8 4.6 collective-permute-done.1
  31.2 3.6 collective-permute-done.3
  35.2 4.8 collective-permute-start
  41.5 4.2 collective-permute-done.1
  45.7 2.9 collective-permute-start.2
  49.9 2.7 collective-permute-done.3
  53.1 2.9 collective-permute-start
  57.5 4.2 collective-permute-done.1
  61.7 3.2 collective-permute-start.2
  69.1 4.8 collective-permute-start
  75.4 4.2 collective-permute-done.1
  79.6 2.9 collective-permute-start.2
  83.8 2.7 collective-permute-done.3
  88.3 117.4 %all-reduce.7.cloned.1.call-done = f32[128,128]{0,1:T(8,128)} async-done(((f32[128,128]{0,1:T(8,128)}), f32[128,128]{0,1:T(8,128)}) %all-reduce.7.cloned.1.call-update) | async-done | bytes 65552 | tf_op jit(solution)/shard_map/psum | solution.py:78
  208.2 122.0 %all-reduce.9.cloned.1.call-done = f32[128,128]{0,1:T(8,128)} async-done(((f32[128,128]{0,1:T(8,128)}), f32[128,128]{0,1:T(8,128)}) %all-reduce.9.cloned.1.call-update) | async-done | bytes 65552 | tf_op jit(solution)/shard_map/psum | solution.py:80
  331.9 11.7 %cholesky.16 = f32[128,128]{1,0:T(8,128)S(1)} custom-call(f32[128,128]{1,0:T(8,128)S(1)} %fusion.24), custom_call_target="Cholesky" | custom-call | tf_op jit(solution)/shard_map/jit(cholesky)/cholesky | solution.py:81
  345.0 9.8 %custom-call.6 = f32[1,128,128]{1,2,0:T(8,128)S(1)} custom-call(f32[1,128,128]{2,1,0:T(8,128)S(1)} %fusion.21), custom_call_target="InvertDiagBlocksLowerTriangular" | custom-call | tf_op jit(solution)/shard_map/triangular_solve | solution.py:83
  356.5 4.5 collective-permute-start.7
  363.8 3.0 collective-permute-start.9
  369.9 36.1 %all-reduce.13.cloned.1.call-done = (f32[128,128]{0,1:T(8,128)}, f32[128,128]{0,1:T(8,128)}) async-done(((f32[128,128]{0,1:T(8,128)}, f32[128,128]{0,1:T(8,128)}), (f32[128,128]{0,1:T(8,128)}, f32[128,128]{0,1:T(8,128)})) %all-reduce.13.cloned.1.call-update) | async-done | bytes 131088 | tf_op jit(solution)/shard_map/psum | solution.py:94
  406.0 73.6 %all-reduce.11.cloned.1.call-done = (f32[128,128]{0,1:T(8,128)}, f32[128,128]{0,1:T(8,128)}) async-done(((f32[128,128]{0,1:T(8,128)}, f32[128,128]{0,1:T(8,128)}), (f32[128,128]{0,1:T(8,128)}, f32[128,128]{0,1:T(8,128)})) %all-reduce.11.cloned.1.call-update) | async-done | bytes 131088 | tf_op jit(solution)/shard_map/psum | solution.py:94
  (109 shorter events, 39.7 us)
Async XLA Ops:
  7.2 198.5 %all-reduce.7.cloned.1.call-start = ((), (), s32[]{:S(2)}) async-start(), calls=%async_computation | async-start | bytes 131072 | tf_op jit(solution)/shard_map/psum | solution.py:78
  7.9 6.9 %collective-permute-start.5 = (f32[16,1]{1,0:T(8,128)S(1)}, f32[16,1]{1,0:T(8,128)S(1)}, u32[]{:S(2)}, u32[]{:S(2)}) collective-permute-start(f32[16,1]{1,0:T(8,128)S(1)} %slice.102), channel_id=1, source_target_pairs={{0,1},{1,2},{2,3},{4,5},{5,6},{6,7},{8,9},{9,10},{10,11},{12,13},{... | collective-permute-start | bytes 200 | tf_op jit(solution)/shard_map/ppermute | solution.py:16
  10.5 5.5 %collective-permute-start.4 = (f32[1,32]{1,0:T(1,128)S(1)}, f32[1,32]{1,0:T(1,128)S(1)}, u32[]{:S(2)}, u32[]{:S(2)}) collective-permute-start(f32[1,32]{1,0:T(1,128)S(1)} %slice.100), channel_id=1, source_target_pairs={{0,4},{4,8},{8,12},{12,16},{16,20},{20,24},{24,28},{1,5},{5,9},{9,... | collective-permute-start | bytes 392 | tf_op jit(solution)/shard_map/ppermute | solution.py:16
  18.1 5.7 %collective-permute-start = (f32[1,32,128]{2,1,0:T(8,128)S(1)}, f32[1,32,128]{2,1,0:T(8,128)S(1)}, u32[]{:S(2)}, u32[]{:S(2)}) collective-permute-start(f32[1,32,128]{2,1,0:T(8,128)S(1)} %get-tuple-element.138), channel_id=1, source_target_pairs={{0,4},{4,8},{8,12},{12,16},{16,20},{20,24},{24,28},{1,5},{5,9},{9,... | collective-permute-start | bytes 49160 | tf_op jit(solution)/shard_map/while/body/eval_jaxpr/ppermute | solution.py:27
  22.4 6.1 %collective-permute-start.1 = (f32[1,32,128]{2,1,0:T(8,128)S(1)}, f32[1,32,128]{2,1,0:T(8,128)S(1)}, u32[]{:S(2)}, u32[]{:S(2)}) collective-permute-start(f32[1,32,128]{2,1,0:T(8,128)S(1)} %get-tuple-element.139), channel_id=1, source_target_pairs={{4,0},{8,4},{12,8},{16,12},{20,16},{24,20},{28,24},{5,1},{9,5},{13... | collective-permute-start | bytes 49160 | tf_op jit(solution)/shard_map/while/body/eval_jaxpr/ppermute | solution.py:29
  29.9 4.9 %collective-permute-start.3 = (f32[18,1,128]{2,1,0:T(1,128)S(1)}, f32[18,1,128]{2,1,0:T(1,128)S(1)}, u32[]{:S(2)}, u32[]{:S(2)}) collective-permute-start(f32[18,1,128]{2,1,0:T(1,128)S(1)} %get-tuple-element.141), channel_id=1, source_target_pairs={{1,0},{2,1},{3,2},{5,4},{6,5},{7,6},{9,8},{10,9},{11,10},{13,12},{... | collective-permute-start | bytes 27656 | tf_op jit(solution)/shard_map/while/body/eval_jaxpr/ppermute | solution.py:29
  35.2 6.3 %collective-permute-start = (f32[1,32,128]{2,1,0:T(8,128)S(1)}, f32[1,32,128]{2,1,0:T(8,128)S(1)}, u32[]{:S(2)}, u32[]{:S(2)}) collective-permute-start(f32[1,32,128]{2,1,0:T(8,128)S(1)} %get-tuple-element.138), channel_id=1, source_target_pairs={{0,4},{4,8},{8,12},{12,16},{16,20},{20,24},{24,28},{1,5},{5,9},{9,... | collective-permute-start | bytes 49160 | tf_op jit(solution)/shard_map/while/body/eval_jaxpr/ppermute | solution.py:27
  40.1 5.6 %collective-permute-start.1 = (f32[1,32,128]{2,1,0:T(8,128)S(1)}, f32[1,32,128]{2,1,0:T(8,128)S(1)}, u32[]{:S(2)}, u32[]{:S(2)}) collective-permute-start(f32[1,32,128]{2,1,0:T(8,128)S(1)} %get-tuple-element.139), channel_id=1, source_target_pairs={{4,0},{8,4},{12,8},{16,12},{20,16},{24,20},{28,24},{5,1},{9,5},{13... | collective-permute-start | bytes 49160 | tf_op jit(solution)/shard_map/while/body/eval_jaxpr/ppermute | solution.py:29
  45.7 4.2 collective-permute-start.2
  48.6 4.0 collective-permute-start.3
  53.1 4.4 collective-permute-start
  56.1 5.6 %collective-permute-start.1 = (f32[1,32,128]{2,1,0:T(8,128)S(1)}, f32[1,32,128]{2,1,0:T(8,128)S(1)}, u32[]{:S(2)}, u32[]{:S(2)}) collective-permute-start(f32[1,32,128]{2,1,0:T(8,128)S(1)} %get-tuple-element.139), channel_id=1, source_target_pairs={{4,0},{8,4},{12,8},{16,12},{20,16},{24,20},{28,24},{5,1},{9,5},{13... | collective-permute-start | bytes 49160 | tf_op jit(solution)/shard_map/while/body/eval_jaxpr/ppermute | solution.py:29
  61.7 4.5 collective-permute-start.2
  69.1 6.3 %collective-permute-start = (f32[1,32,128]{2,1,0:T(8,128)S(1)}, f32[1,32,128]{2,1,0:T(8,128)S(1)}, u32[]{:S(2)}, u32[]{:S(2)}) collective-permute-start(f32[1,32,128]{2,1,0:T(8,128)S(1)} %get-tuple-element.138), channel_id=1, source_target_pairs={{0,4},{4,8},{8,12},{12,16},{16,20},{20,24},{24,28},{1,5},{5,9},{9,... | collective-permute-start | bytes 49160 | tf_op jit(solution)/shard_map/while/body/eval_jaxpr/ppermute | solution.py:27
  73.9 5.6 %collective-permute-start.1 = (f32[1,32,128]{2,1,0:T(8,128)S(1)}, f32[1,32,128]{2,1,0:T(8,128)S(1)}, u32[]{:S(2)}, u32[]{:S(2)}) collective-permute-start(f32[1,32,128]{2,1,0:T(8,128)S(1)} %get-tuple-element.139), channel_id=1, source_target_pairs={{4,0},{8,4},{12,8},{16,12},{20,16},{24,20},{28,24},{5,1},{9,5},{13... | collective-permute-start | bytes 49160 | tf_op jit(solution)/shard_map/while/body/eval_jaxpr/ppermute | solution.py:29
  79.6 4.2 collective-permute-start.2
  82.5 4.0 collective-permute-start.3
  88.2 242.0 %all-reduce.9.cloned.1.call-start = ((), (), s32[]{:S(2)}) async-start(), calls=%async_computation.1 | async-start | bytes 131072 | tf_op jit(solution)/shard_map/psum | solution.py:80
  208.2 197.8 %all-reduce.13.cloned.1.call-start = ((), (), s32[]{:S(2)}) async-start(), calls=%async_computation.3 | async-start | bytes 262144 | tf_op jit(solution)/shard_map/psum | solution.py:94
  355.2 5.9 %collective-permute-start.6 = (f32[1,32,128]{2,1,0:T(8,128)S(1)}, f32[1,32,128]{2,1,0:T(8,128)S(1)}, u32[]{:S(2)}, u32[]{:S(2)}) collective-permute-start(f32[1,32,128]{2,1,0:T(8,128)S(1)} %get-tuple-element.82), channel_id=1, source_target_pairs={{4,0},{8,4},{12,8},{16,12},{20,16},{24,20},{28,24},{5,1},{9,5},{13... | collective-permute-start | bytes 49160 | tf_op jit(solution)/shard_map/ppermute | solution.py:29
  356.5 6.0 %collective-permute-start.7 = (f32[1,32,128]{2,1,0:T(8,128)S(1)}, f32[1,32,128]{2,1,0:T(8,128)S(1)}, u32[]{:S(2)}, u32[]{:S(2)}) collective-permute-start(f32[1,32,128]{2,1,0:T(8,128)S(1)} %get-tuple-element.81), channel_id=1, source_target_pairs={{0,4},{4,8},{8,12},{12,16},{16,20},{20,24},{24,28},{1,5},{5,9},{9,... | collective-permute-start | bytes 49160 | tf_op jit(solution)/shard_map/ppermute | solution.py:27
  362.5 5.7 %collective-permute-start.8 = (f32[18,1,128]{2,1,0:T(1,128)S(1)}, f32[18,1,128]{2,1,0:T(1,128)S(1)}, u32[]{:S(2)}, u32[]{:S(2)}) collective-permute-start(f32[18,1,128]{2,1,0:T(1,128)S(1)} %get-tuple-element.79), channel_id=1, source_target_pairs={{1,0},{2,1},{3,2},{5,4},{6,5},{7,6},{9,8},{10,9},{11,10},{13,12},{... | collective-permute-start | bytes 27656 | tf_op jit(solution)/shard_map/ppermute | solution.py:29
  363.8 4.4 collective-permute-start.9
  369.8 109.8 %all-reduce.11.cloned.1.call-start = ((), (), s32[]{:S(2)}) async-start(), calls=%async_computation.2 | async-start | bytes 262144 | tf_op jit(solution)/shard_map/psum | solution.py:94
  (10 other events, 96.1 us)
Sparse Core Ops, SparseCore 0:
  88.3 117.3 all-reduce.6
  211.8 118.3 all-reduce.8
  369.9 35.9 all-reduce.12
  409.7 69.8 all-reduce.10
